TPU v7x, 128 devices: a whole 4x4x4 slice. The times are simulated.
128 devices in a mesh: blk: 16 (over z_lo, y, core), group: 8 (over x, z_hi).
Axes of the slice: x: 4, y: 4, z: 4 (z_hi: 2, z_lo: 2; z = z_hi * 2 + z_lo), core: 2. Of those that a mesh axis runs over, the one named last changes fastest.
Arguments:
- centres: bfloat16 [262144, 1024], P(('blk', 'group')), may hold values from -8 to 8
- batch_x: bfloat16 [2048, 1024], P(('blk', 'group')), may hold values from -8 to 8
- grad: bfloat16 [2048, 1000], P(('blk', 'group')), may hold values from -0.29882812 to 0.29882812
- eigvec: float32 [65536, 128], P(('blk', 'group')), may hold values from -0.0234375 to 0.0234375
- eig_scale: float32 [128], replicated, may hold values from 2 to 20
- sub_index: int32 [65536], P(('blk', 'group')), may hold values from 0 to 262143, as said below
Outputs:
- update: float32 [262144, 1000], P(('blk', 'group'))
Inputs may be any that keep to these rules, and one draw needn't show every extreme that they name: `sub_index`: all entries are distinct. Entry i of the block of 512 entries that device index k of blk+group holds names a centre among rows (k // 8) * 8 * 2048 to (k // 8 + 1) * 8 * 2048 - 1; among one such block at most 128 entries name rows of any one aligned run of 2048 centres, and every block has exactly 128 in one run.
All inputs are finite; a program needn't handle non-finite values.
Results may differ from a plain program's by a relative error of at most 0.0027.
Values may be sent and summed in bfloat16 or wider, within the bound.
No kernel may reach another device: no remote copies, remote signals or barrier semaphores. Data moves between devices by JAX's collectives and lax.ppermute only.
A program may use at most 128 MiB of HBM per device.

v0:
```python
import jax
import jax.numpy as jnp
from jax import lax
from jax.sharding import PartitionSpec as P

D = 1024
CAP = 128


def scatter_sum(value, axis):
    size = lax.axis_size(axis)
    got = lax.all_to_all(value, axis, split_axis=0, concat_axis=0, tiled=True)
    return got.reshape((size, -1) + value.shape[1:]).sum(axis=0)


def gather_back(value, axis):
    size = lax.axis_size(axis)
    return lax.all_to_all(jnp.tile(value, (size, 1)), axis, split_axis=0, concat_axis=0, tiled=True)


def tree_psum(value):
    part = scatter_sum(scatter_sum(value, "group"), "blk")
    return gather_back(gather_back(part, "blk"), "group")


def body(centres, batch_x, grad, eigvec, eig_scale, sub_index):
    dims = batch_x.shape[1]
    centre_sq = jnp.sum(jnp.square(centres.astype(jnp.float32)), axis=1)
    joined = jnp.concatenate([batch_x, grad], axis=1)
    joined = gather_back(joined, "group")
    joined = lax.all_gather(joined, "blk", axis=0, tiled=True)
    piece_x = joined[:, :dims]
    piece_g = joined[:, dims:]
    batch_sq = jnp.sum(jnp.square(piece_x.astype(jnp.float32)), axis=1)
    inner_prod = jnp.einsum("cd,bd->cb", centres, piece_x, preferred_element_type=jnp.float32)
    distance = centre_sq[:, None] + batch_sq[None, :] - 2.0 * inner_prod
    kernel_tile = jnp.exp(-distance / (2.0 * D)).astype(jnp.bfloat16)
    kernel_grad = jnp.dot(kernel_tile, piece_g, preferred_element_type=jnp.float32)
    groups = lax.axis_size("group")
    rows_each = centres.shape[0]
    holder = sub_index // rows_each % groups
    local_row = sub_index % rows_each
    onehot = (holder[:, None] == jnp.arange(groups, dtype=jnp.int32)[None, :]).astype(jnp.int32)
    order_in = jnp.sum(jnp.cumsum(onehot, axis=0) * onehot, axis=1) - 1
    position = holder * CAP + order_in
    slot_table = jnp.zeros((groups * CAP,), jnp.int32).at[position].set(local_row)
    eig_table = jnp.zeros((groups * CAP, eigvec.shape[1]), jnp.float32).at[position].set(eigvec)
    got_slots = lax.all_to_all(slot_table, "group", split_axis=0, concat_axis=0, tiled=True)
    got_eig = lax.all_to_all(eig_table, "group", split_axis=0, concat_axis=0, tiled=True)
    sub_rows = centres[got_slots]
    sub_inner = jnp.einsum("cd,bd->cb", sub_rows, piece_x, preferred_element_type=jnp.float32)
    sub_distance = centre_sq[got_slots][:, None] + batch_sq[None, :] - 2.0 * sub_inner
    sub_tile = jnp.exp(-sub_distance / (2.0 * D)).astype(jnp.bfloat16)
    picked = jnp.dot(sub_tile, piece_g, preferred_element_type=jnp.float32)
    partial = jnp.einsum("sq,sk->qk", got_eig, picked, precision=lax.Precision.HIGH)
    projected = tree_psum(partial)
    correction = jnp.dot(got_eig * eig_scale[None, :], projected, precision=lax.Precision.HIGH)
    rounded = lax.reduce_precision(correction, exponent_bits=8, mantissa_bits=7)
    upper = rounded.astype(jnp.bfloat16)
    lower = (correction - rounded).astype(jnp.bfloat16)
    hits = (jnp.arange(rows_each, dtype=jnp.int32)[:, None] == got_slots[None, :]).astype(jnp.bfloat16)
    placed = jnp.dot(
        jnp.concatenate([hits, hits], axis=1),
        jnp.concatenate([upper, lower], axis=0),
        preferred_element_type=jnp.float32,
    )
    return kernel_grad - placed


def solution(mesh):
    in_specs = (
        P(("blk", "group"), None),
        P(("blk", "group"), None),
        P(("blk", "group"), None),
        P(("blk", "group"), None),
        P(),
        P(("blk", "group")),
    )
    out_specs = P(("blk", "group"), None)
    return jax.shard_map(body, mesh=mesh, in_specs=in_specs, out_specs=out_specs, check_vma=False)
```

profile of v0, /device:TPU:1, one launch (start us, length us, event | category | flops | bytes accessed | tf_op | source)
XLA Modules:
  0.0 202.9 jit_solution(18324133550610219978)
XLA Ops:
  6.5 0.8 pad_maximum_fusion
  7.4 17.8 %all_to_all.63 = bf16[8,16,2024]{2,1,0:T(8,128)(2,1)} all-to-all(bf16[8,16,2024]{2,1,0:T(8,128)(2,1)S(1)} %tile.8), channel_id=1, replica_groups=mesh['blk'=16,'group'=8] {'group'}, dimensions={0} | all-to-all | bytes 1036288 | tf_op jit(solution)/shard_map/all_to_all | solution.py:18
  25.2 0.0 all-gather.2.cloned.1.call-update
  25.2 0.7 add_select_fusion
  25.9 1.1 reduce-window.6
  27.1 0.2 slice_reduce_fusion
  27.3 0.1 fusion.30
  27.4 3.0 %scatter_custom_fusion = s32[1024]{0:T(1024)} fusion(s32[512]{0:T(512)S(1)} %compare_select_fusion.1, s32[512]{0:T(512)S(1)} %get-tuple-element.7, s32[]{:T(128)} %constant.54.clone.1), kind=kCustom, calls=%fused_computation.60 | custom fusion | bytes 4100 | tf_op jit(solution)/shard_map/scatter | solution.py:46
  30.4 3.4 %all-to-all-start.1 = ((s32[8,128,1]{1,2,0:T(1,128)}), s32[8,128,1]{1,2,0:T(1,128)S(1)}, u32[]{:S(2)}, u32[]{:S(2)}) async-start(s32[8,128,1]{1,2,0:T(1,128)} %bitcast.6), calls=%async_computation.1 | async-start | bytes 8192 | tf_op jit(solution)/shard_map/all_to_all | solution.py:48
  33.9 2.9 %scatter_custom_fusion.1 = f32[1024,128]{1,0:T(8,128)} fusion(s32[512]{0:T(512)S(1)} %compare_select_fusion.1, f32[512,128]{1,0:T(8,128)} %param.9, f32[]{:T(128)} %constant.51.clone.1), kind=kCustom, calls=%fused_computation.37 | custom fusion | bytes 524800 | tf_op jit(solution)/shard_map/scatter | solution.py:47
  36.8 3.5 %all-to-all-done.1 = s32[8,128,1]{1,2,0:T(1,128)S(1)} async-done(((s32[8,128,1]{1,2,0:T(1,128)}), s32[8,128,1]{1,2,0:T(1,128)S(1)}, u32[]{:S(2)}, u32[]{:S(2)}) %all-to-all-start.1) | async-done | bytes 4128 | tf_op jit(solution)/shard_map/all_to_all | solution.py:48
  40.3 3.5 %all-to-all-start.2 = ((f32[8,128,128]{2,1,0:T(8,128)}), f32[8,128,128]{2,1,0:T(8,128)S(1)}, u32[]{:S(2)}, u32[]{:S(2)}) async-start(f32[8,128,128]{2,1,0:T(8,128)} %bitcast.8), calls=%async_computation.2 | async-start | bytes 1048576 | tf_op jit(solution)/shard_map/all_to_all | solution.py:49
  43.8 3.2 %multiply_reduce_fusion.1 = f32[2048]{0:T(1024)S(1)} fusion(bf16[2048,1024]{1,0:T(8,128)(2,1)} %param.6), kind=kLoop, calls=%fused_computation.21 | loop fusion | flops 6289408 | bytes 4202496 | tf_op jit(solution)/shard_map/reduce_sum | solution.py:28
  46.9 7.7 %gather_fusion.1 = bf16[1024,1024]{1,0:T(8,128)(2,1)S(1)} fusion(bf16[2048,1024]{1,0:T(8,128)(2,1)} %param.6, s32[1024]{0:T(1024)S(1)} %broadcast_clamp_fusion), kind=kCustom, calls=%fused_computation.1 | custom fusion | bytes 4198400 | tf_op jit(solution)/shard_map/gather | solution.py:50
  54.7 6.3 %gather_fusion = f32[1024]{0:T(1024)S(1)} fusion(f32[2048]{0:T(1024)S(1)} %multiply_reduce_fusion.1, s32[1024]{0:T(1024)S(1)} %broadcast_clamp_fusion), kind=kCustom, calls=%fused_computation | custom fusion | bytes 12288 | tf_op jit(solution)/shard_map/gather | solution.py:52
  61.0 0.2 copy.12
  61.2 21.9 %all-gather.2.cloned.1.call-done = bf16[2048,2024]{1,0:T(8,128)(2,1)} async-done(((bf16[128,2024]{1,0:T(8,128)(2,1)}), bf16[2048,2024]{1,0:T(8,128)(2,1)}) %all-gather.2.cloned.1.call-update) | async-done | bytes 8290320 | tf_op jit(solution)/shard_map/all_gather | solution.py:31
  83.1 3.1 %multiply_reduce_fusion = f32[2048]{0:T(1024)S(1)} fusion(bf16[2048,2024]{1,0:T(8,128)(2,1)} %all-gather.2.cloned.1.call-done), kind=kLoop, calls=%fused_computation.19 | loop fusion | flops 6289408 | bytes 4202496 | tf_op jit(solution)/shard_map/reduce_sum | solution.py:34
  86.2 14.8 %fusion.20 = f32[1024,1000]{0,1:T(8,128)} fusion(bf16[2048,2024]{1,0:T(8,128)(2,1)} %all-gather.2.cloned.1.call-done, bf16[1024,1024]{1,0:T(8,128)(2,1)S(1)} %gather_fusion.1, f32[2048]{0:T(1024)S(1)} %multiply_reduce_fusion, f32[1024]{0:T(1024)S(1)} %gather_fusion), kind=kOutput, calls=%fused_computation.31 | convolution fusion | flops 8501854208 | bytes 14495744 | tf_op jit(solution)/shard_map/dot_general | solution.py:54
  101.0 4.0 %fusion.18 = f32[8,16,1000]{2,1,0:T(8,128)S(1)} fusion(f32[8,16,1024]{2,1,0:T(8,128)S(1)} %bitcast.51, f32[1024,1000]{0,1:T(8,128)} %fusion.20), kind=kOutput, calls=%fused_computation.29 | convolution fusion | flops 786432000 | bytes 5132288 | tf_op jit(solution)/shard_map/sq,sk->qk/dot_general | solution.py:55
  105.1 0.0 copy-start.1
  105.1 16.1 %all_to_all.64 = f32[8,16,1000]{2,1,0:T(8,128)S(1)} all-to-all(f32[8,16,1000]{2,1,0:T(8,128)S(1)} %fusion.18), channel_id=1, replica_groups=mesh['blk'=16,'group'=8] {'group'}, dimensions={0} | all-to-all | bytes 1024000 | tf_op jit(solution)/shard_map/all_to_all | solution.py:12
  121.3 11.7 %all_to_all.65 = f32[16,1,1000]{2,1,0:T(1,128)S(1)} all-to-all(f32[16,1,1000]{2,1,0:T(1,128)S(1)} %all_to_all.51), channel_id=1, replica_groups=mesh['blk'=16,'group'=8] {'blk'}, dimensions={0} | all-to-all | bytes 128000 | tf_op jit(solution)/shard_map/all_to_all | solution.py:12
  133.0 0.1 reduce_sum.49
  133.1 8.7 %all_to_all.66 = f32[16,1,1000]{2,1,0:T(1,128)S(1)} all-to-all(f32[16,1,1000]{2,1,0:T(1,128)S(1)} %tile.9), channel_id=1, replica_groups=mesh['blk'=16,'group'=8] {'blk'}, dimensions={0} | all-to-all | bytes 128000 | tf_op jit(solution)/shard_map/all_to_all | solution.py:18
  141.8 0.9 tile.11
  142.7 3.5 %all-to-all-start.6 = ((f32[8,16,1000]{2,1,0:T(8,128)}), f32[8,16,1000]{2,1,0:T(8,128)S(1)}, u32[]{:S(2)}, u32[]{:S(2)}) async-start(f32[8,16,1000]{2,1,0:T(8,128)} %tile.11), calls=%async_computation.6 | async-start | bytes 1048576 | tf_op jit(solution)/shard_map/all_to_all | solution.py:18
  146.2 3.1 %iota_compare_fusion = pred[2048,1024]{1,0:T(32,128)(4,1)} fusion(s32[1024]{0:T(1024)S(1)} %bitcast.55), kind=kLoop, calls=%fused_computation.15 | loop fusion | flops 2097152 | bytes 2101248 | tf_op jit(solution)/shard_map/eq | solution.py:61
  149.3 7.3 %all-to-all-done.6 = f32[8,16,1000]{2,1,0:T(8,128)S(1)} async-done(((f32[8,16,1000]{2,1,0:T(8,128)}), f32[8,16,1000]{2,1,0:T(8,128)S(1)}, u32[]{:S(2)}, u32[]{:S(2)}) %all-to-all-start.6) | async-done | bytes 512032 | tf_op jit(solution)/shard_map/all_to_all | solution.py:18
  156.7 2.0 reduce-precision_convert_fusion
  158.7 10.9 %fusion.4 = f32[2048,1000]{0,1:T(8,128)} fusion(pred[2048,1024]{1,0:T(32,128)(4,1)S(1)} %copy-done, bf16[1024,1000]{0,1:T(8,128)(2,1)S(1)} %get-tuple-element.6, bf16[1024,1000]{0,1:T(8,128)(2,1)S(1)} %get-tuple-element.5), kind=kOutput, calls=%fused_computation.9 | convolution fusion | flops 8400994304 | bytes 14385152 | tf_op jit(solution)/shard_map/dot_general | solution.py:62
  169.6 26.5 %fusion.13 = f32[2048,1000]{0,1:T(8,128)} fusion(f32[2048,1000]{0,1:T(8,128)} %fusion.4, bf16[2048,1024]{1,0:T(8,128)(2,1)} %param.6, f32[2048]{0:T(1024)S(1)} %multiply_reduce_fusion, f32[2048]{0:T(1024)S(1)} %multiply_reduce_fusion.1, bf16[2048,2024]{1,0:T(8,128)(2,1)} %all-gather.2.cloned.1.call-done), kind=kOutput, calls=%fused_computation.24 | convolution fusion | flops 17005756416 | bytes 28884992 | tf_op jit(solution)/shard_map/dot_general | solution.py:38
  (17 shorter events, 0.3 us)
Async XLA Ops:
  6.5 76.6 %all-gather.2.cloned.1.call-start = ((), (), s32[]{:S(2)}) async-start(), calls=%async_computation.7 | async-start | bytes 8912896 | tf_op jit(solution)/shard_map/all_gather | solution.py:31
  30.4 9.8 %all-to-all-start.1 = ((s32[8,128,1]{1,2,0:T(1,128)}), s32[8,128,1]{1,2,0:T(1,128)S(1)}, u32[]{:S(2)}, u32[]{:S(2)}) async-start(s32[8,128,1]{1,2,0:T(1,128)} %bitcast.6), calls=%async_computation.1 | async-start | bytes 8192 | tf_op jit(solution)/shard_map/all_to_all | solution.py:48
  40.3 20.8 %all-to-all-start.2 = ((f32[8,128,128]{2,1,0:T(8,128)}), f32[8,128,128]{2,1,0:T(8,128)S(1)}, u32[]{:S(2)}, u32[]{:S(2)}) async-start(f32[8,128,128]{2,1,0:T(8,128)} %bitcast.8), calls=%async_computation.2 | async-start | bytes 1048576 | tf_op jit(solution)/shard_map/all_to_all | solution.py:49
  105.1 44.2 %copy-start.1 = (f32[128]{0:T(128)S(1)}, f32[128]{0:T(128)}, u32[]{:S(2)}) copy-start(f32[128]{0:T(128)} %param.10) | copy-start | bytes 1540
  142.7 14.0 %all-to-all-start.6 = ((f32[8,16,1000]{2,1,0:T(8,128)}), f32[8,16,1000]{2,1,0:T(8,128)S(1)}, u32[]{:S(2)}, u32[]{:S(2)}) async-start(f32[8,16,1000]{2,1,0:T(8,128)} %tile.11), calls=%async_computation.6 | async-start | bytes 1048576 | tf_op jit(solution)/shard_map/all_to_all | solution.py:18
  156.7 2.0 copy-start
Sparse Core Ops, SparseCore 0:
  25.3 57.7 all-gather.1
where the time goes:
time: 204 us; the launch traced here: 203 us
  matrix products  58.2 us (29%)
  blocking collectives  54.3 us (27%)
  waiting for transfers between devices  32.7 us (16%)
  local copies, waits for them, and re-layouts  21.4 us (10%)
  between operations  13.5 us (7%)
  other arithmetic  12.2 us (6%)
  starting transfers between devices  10.4 us (5%)
    all_to_all x2, blocking collectives, scatter_sum(): got = lax.all_to_all(value, axis, split_axis=0, concat_axis=0, tiled=True)  27.8 us
    all_to_all x2, blocking collectives, gather_back(): lax.all_to_all(jnp.tile(value, (size, 1)), axis, split_axis=0, concat_axi...  26.5 us
    dot_general x1, matrix products, body(): jnp.dot(kernel_tile, piece_g, preferred_element_type=jnp.float32)  26.5 us
    all_gather x1, waiting for transfers between devices, body(): joined = lax.all_gather(joined, 'blk', axis=0, tiled=True)  21.9 us
    dot_general x1, matrix products, body(): picked = jnp.dot(sub_tile, piece_g, preferred_element_type=jnp.float32)  14.8 us
    dot_general x1, matrix products, body(): jnp.dot(jnp.concatenate([hits, hits], axis=1), jnp.concatenate([upper, lo...  10.9 us
    gather x1, local copies, waits for them, and re-layouts, body(): sub_rows = centres[got_slots]  7.71 us
    all_to_all x1, waiting for transfers between devices, gather_back(): lax.all_to_all(jnp.tile(value, (size, 1)), axis, split_axis=0, concat_axi...  7.34 us
  transfers between devices with their start and end apart: 4, of which 3 were waited for; matrix products, arithmetic and copies ran while one was open for 14% of the time, Pallas kernels for 0%

commit v1 on v0

--- a/solution.py
+++ b/solution.py
@@ -35,7 +35,9 @@
     inner_prod = jnp.einsum("cd,bd->cb", centres, piece_x, preferred_element_type=jnp.float32)
     distance = centre_sq[:, None] + batch_sq[None, :] - 2.0 * inner_prod
     kernel_tile = jnp.exp(-distance / (2.0 * D)).astype(jnp.bfloat16)
-    kernel_grad = jnp.dot(kernel_tile, piece_g, preferred_element_type=jnp.float32)
+    kernel_grad = lax.optimization_barrier(
+        jnp.dot(kernel_tile, piece_g, preferred_element_type=jnp.float32)
+    )
     groups = lax.axis_size("group")
     rows_each = centres.shape[0]
     holder = sub_index // rows_each % groups

time: 204 us -> 197 us (0.966)
  blocking collectives: 54.3 us -> 33.9 us
  starting transfers between devices: 10.4 us -> 20.2 us
  waiting for transfers between devices: 32.7 us -> 35.3 us
    all_to_all x2 -> x1, blocking collectives: 27.8 us -> 16.1 us  [scatter_sum(): got = lax.all_to_all(value, axis, split_axis=0, concat_axis=0, tiled=True)]
    all_to_all x2 -> x1, blocking collectives: 26.5 us -> 17.8 us  [gather_back(): lax.all_to_all(jnp.tile(value, (size, 1)), axis, split_axis=0, concat_axi...]
    all_to_all x0 -> x1, starting transfers between devices: none -> 6.09 us  [scatter_sum(): got = lax.all_to_all(value, axis, split_axis=0, concat_axis=0, tiled=True)]
    all_to_all x0 -> x1, waiting for transfers between devices: none -> 4.03 us  [scatter_sum(): got = lax.all_to_all(value, axis, split_axis=0, concat_axis=0, tiled=True)]
    all_to_all x1 -> x2, starting transfers between devices: 3.49 us -> 7.18 us  [gather_back(): lax.all_to_all(jnp.tile(value, (size, 1)), axis, split_axis=0, concat_axi...]
    dot_general x1, matrix products: 10.9 us -> 13.3 us  [body(): jnp.dot(jnp.concatenate([hits, hits], axis=1), jnp.concatenate([upper, lo...]
    all_to_all x1 -> x2, waiting for transfers between devices: 7.34 us -> 5.84 us  [gather_back(): lax.all_to_all(jnp.tile(value, (size, 1)), axis, split_axis=0, concat_axi...]
  transfers between devices with their start and end apart: 4 -> 6, of which waited for: 3 -> 4; matrix products, arithmetic and copies ran while one was open for 14% -> 27% of each run, Pallas kernels for 0% -> 0%
where the time goes in v1:
time: 197 us; the launch traced here: 196 us
  matrix products  59.5 us (30%)
  waiting for transfers between devices  35.3 us (18%)
  blocking collectives  33.9 us (17%)
  local copies, waits for them, and re-layouts  22.7 us (12%)
  starting transfers between devices  20.2 us (10%)
  between operations  13.5 us (7%)
  other arithmetic  10.9 us (6%)
    dot_general x1, matrix products, body(): jnp.dot(kernel_tile, piece_g, preferred_element_type=jnp.float32)  25.3 us
    all_gather x1, waiting for transfers between devices, body(): joined = lax.all_gather(joined, 'blk', axis=0, tiled=True)  21.9 us
    all_to_all x1, blocking collectives, gather_back(): lax.all_to_all(jnp.tile(value, (size, 1)), axis, split_axis=0, concat_axi...  17.8 us
    all_to_all x1, blocking collectives, scatter_sum(): got = lax.all_to_all(value, axis, split_axis=0, concat_axis=0, tiled=True)  16.1 us
    dot_general x1, matrix products, body(): picked = jnp.dot(sub_tile, piece_g, preferred_element_type=jnp.float32)  14.8 us
    dot_general x1, matrix products, body(): jnp.dot(jnp.concatenate([hits, hits], axis=1), jnp.concatenate([upper, lo...  13.3 us
    gather x1, local copies, waits for them, and re-layouts, body(): sub_rows = centres[got_slots]  7.71 us
    all_to_all x2, starting transfers between devices, gather_back(): lax.all_to_all(jnp.tile(value, (size, 1)), axis, split_axis=0, concat_axi...  7.18 us
  transfers between devices with their start and end apart: 6, of which 4 were waited for; matrix products, arithmetic and copies ran while one was open for 27% of the time, Pallas kernels for 0%

profile of v1, /device:TPU:1, one launch (start us, length us, event | category | flops | bytes accessed | tf_op | source)
XLA Modules:
  0.0 196.0 jit_solution(7433111822574480883)
XLA Ops:
  6.5 0.8 pad_maximum_fusion
  7.4 17.8 %all_to_all.63 = bf16[8,16,2024]{2,1,0:T(8,128)(2,1)} all-to-all(bf16[8,16,2024]{2,1,0:T(8,128)(2,1)S(1)} %tile.8), channel_id=1, replica_groups=mesh['blk'=16,'group'=8] {'group'}, dimensions={0} | all-to-all | bytes 1036288 | tf_op jit(solution)/shard_map/all_to_all | solution.py:18
  25.2 0.7 add_select_fusion
  25.9 1.1 reduce-window.6
  27.1 0.2 slice_reduce_fusion
  27.3 0.1 fusion.34
  27.4 3.0 %scatter_custom_fusion = s32[1024]{0:T(1024)} fusion(s32[512]{0:T(512)S(1)} %compare_select_fusion.1, s32[512]{0:T(512)S(1)} %get-tuple-element.7, s32[]{:T(128)} %constant.54.clone.1), kind=kCustom, calls=%fused_computation.60 | custom fusion | bytes 4100 | tf_op jit(solution)/shard_map/scatter | solution.py:48
  30.4 3.4 %all-to-all-start.1 = ((s32[8,128,1]{1,2,0:T(1,128)}), s32[8,128,1]{1,2,0:T(1,128)S(1)}, u32[]{:S(2)}, u32[]{:S(2)}) async-start(s32[8,128,1]{1,2,0:T(1,128)} %bitcast.6), calls=%async_computation.1 | async-start | bytes 8192 | tf_op jit(solution)/shard_map/all_to_all | solution.py:50
  33.9 2.9 %scatter_custom_fusion.1 = f32[1024,128]{1,0:T(8,128)} fusion(s32[512]{0:T(512)S(1)} %compare_select_fusion.1, f32[512,128]{1,0:T(8,128)} %param.9, f32[]{:T(128)} %constant.51.clone.1), kind=kCustom, calls=%fused_computation.37 | custom fusion | bytes 524800 | tf_op jit(solution)/shard_map/scatter | solution.py:49
  36.8 3.5 %all-to-all-done.1 = s32[8,128,1]{1,2,0:T(1,128)S(1)} async-done(((s32[8,128,1]{1,2,0:T(1,128)}), s32[8,128,1]{1,2,0:T(1,128)S(1)}, u32[]{:S(2)}, u32[]{:S(2)}) %all-to-all-start.1) | async-done | bytes 4128 | tf_op jit(solution)/shard_map/all_to_all | solution.py:50
  40.3 3.5 %all-to-all-start.2 = ((f32[8,128,128]{2,1,0:T(8,128)}), f32[8,128,128]{2,1,0:T(8,128)S(1)}, u32[]{:S(2)}, u32[]{:S(2)}) async-start(f32[8,128,128]{2,1,0:T(8,128)} %bitcast.8), calls=%async_computation.2 | async-start | bytes 1048576 | tf_op jit(solution)/shard_map/all_to_all | solution.py:51
  43.8 3.2 %multiply_reduce_fusion.1 = f32[2048]{0:T(1024)S(1)} fusion(bf16[2048,1024]{1,0:T(8,128)(2,1)} %param.6), kind=kLoop, calls=%fused_computation.21 | loop fusion | flops 6289408 | bytes 4202496 | tf_op jit(solution)/shard_map/reduce_sum | solution.py:28
  46.9 7.7 %gather_fusion.1 = bf16[1024,1024]{1,0:T(8,128)(2,1)S(1)} fusion(bf16[2048,1024]{1,0:T(8,128)(2,1)} %param.6, s32[1024]{0:T(1024)S(1)} %broadcast_clamp_fusion), kind=kCustom, calls=%fused_computation.1 | custom fusion | bytes 4198400 | tf_op jit(solution)/shard_map/gather | solution.py:52
  54.7 6.3 %gather_fusion = f32[1024]{0:T(1024)S(1)} fusion(f32[2048]{0:T(1024)S(1)} %multiply_reduce_fusion.1, s32[1024]{0:T(1024)S(1)} %broadcast_clamp_fusion), kind=kCustom, calls=%fused_computation | custom fusion | bytes 12288 | tf_op jit(solution)/shard_map/gather | solution.py:54
  61.0 0.2 copy.12
  61.2 21.9 %all-gather.2.cloned.1.call-done = bf16[2048,2024]{1,0:T(8,128)(2,1)} async-done(((bf16[128,2024]{1,0:T(8,128)(2,1)}), bf16[2048,2024]{1,0:T(8,128)(2,1)}) %all-gather.2.cloned.1.call-update) | async-done | bytes 8290320 | tf_op jit(solution)/shard_map/all_gather | solution.py:31
  83.1 3.1 %multiply_reduce_fusion = f32[2048]{0:T(1024)S(1)} fusion(bf16[2048,2024]{1,0:T(8,128)(2,1)} %all-gather.2.cloned.1.call-done), kind=kLoop, calls=%fused_computation.19 | loop fusion | flops 6289408 | bytes 4202496 | tf_op jit(solution)/shard_map/reduce_sum | solution.py:34
  86.2 14.8 %fusion.24 = f32[1024,1000]{0,1:T(8,128)} fusion(bf16[2048,2024]{1,0:T(8,128)(2,1)} %all-gather.2.cloned.1.call-done, bf16[1024,1024]{1,0:T(8,128)(2,1)S(1)} %gather_fusion.1, f32[2048]{0:T(1024)S(1)} %multiply_reduce_fusion, f32[1024]{0:T(1024)S(1)} %gather_fusion), kind=kOutput, calls=%fused_computation.31 | convolution fusion | flops 8501854208 | bytes 14495744 | tf_op jit(solution)/shard_map/dot_general | solution.py:56
  101.0 4.1 %fusion.22 = f32[8,16,1000]{2,1,0:T(8,128)S(1)} fusion(f32[8,16,1024]{2,1,0:T(8,128)S(1)} %bitcast.49, f32[1024,1000]{0,1:T(8,128)} %fusion.24), kind=kOutput, calls=%fused_computation.29 | convolution fusion | flops 786432000 | bytes 5132288 | tf_op jit(solution)/shard_map/sq,sk->qk/dot_general | solution.py:57
  105.1 16.1 %all_to_all.64 = f32[8,16,1000]{2,1,0:T(8,128)S(1)} all-to-all(f32[8,16,1000]{2,1,0:T(8,128)S(1)} %fusion.22), channel_id=1, replica_groups=mesh['blk'=16,'group'=8] {'group'}, dimensions={0} | all-to-all | bytes 1024000 | tf_op jit(solution)/shard_map/all_to_all | solution.py:12
  121.2 0.7 all_to_all.51
  121.9 6.1 %all-to-all-start.4 = ((f32[16,1,1000]{2,1,0:T(1,128)}), f32[16,1,1000]{2,1,0:T(1,128)S(1)}, u32[]{:S(2)}, u32[]{:S(2)}) async-start(f32[16,1,1000]{2,1,0:T(1,128)} %all_to_all.51), calls=%async_computation.4 | async-start | bytes 131072 | tf_op jit(solution)/shard_map/all_to_all | solution.py:12
  127.9 1.8 iota_compare_fusion
  129.7 4.0 %all-to-all-done.4 = f32[16,1,1000]{2,1,0:T(1,128)S(1)} async-done(((f32[16,1,1000]{2,1,0:T(1,128)}), f32[16,1,1000]{2,1,0:T(1,128)S(1)}, u32[]{:S(2)}, u32[]{:S(2)}) %all-to-all-start.4) | async-done | bytes 64032 | tf_op jit(solution)/shard_map/all_to_all | solution.py:12
  133.8 0.7 tile.9
  134.5 3.7 %all-to-all-start.5 = ((f32[16,1,1000]{2,1,0:T(1,128)}), f32[16,1,1000]{2,1,0:T(1,128)S(1)}, u32[]{:S(2)}, u32[]{:S(2)}) async-start(f32[16,1,1000]{2,1,0:T(1,128)} %tile.9), calls=%async_computation.5 | async-start | bytes 131072 | tf_op jit(solution)/shard_map/all_to_all | solution.py:18
  138.2 5.8 %all-to-all-done.5 = f32[16,1,1000]{2,1,0:T(1,128)S(1)} async-done(((f32[16,1,1000]{2,1,0:T(1,128)}), f32[16,1,1000]{2,1,0:T(1,128)S(1)}, u32[]{:S(2)}, u32[]{:S(2)}) %all-to-all-start.5) | async-done | bytes 64032 | tf_op jit(solution)/shard_map/all_to_all | solution.py:18
  144.1 0.9 tile.11
  145.0 3.5 %all-to-all-start.6 = ((f32[8,16,1000]{2,1,0:T(8,128)}), f32[8,16,1000]{2,1,0:T(8,128)S(1)}, u32[]{:S(2)}, u32[]{:S(2)}) async-start(f32[8,16,1000]{2,1,0:T(8,128)} %tile.11), calls=%async_computation.6 | async-start | bytes 1048576 | tf_op jit(solution)/shard_map/all_to_all | solution.py:18
  148.5 25.3 %fusion.8 = f32[2048,1000]{0,1:T(8,128)} fusion(bf16[2048,1024]{1,0:T(8,128)(2,1)} %param.6, f32[2048]{0:T(1024)S(1)} %multiply_reduce_fusion, f32[2048]{0:T(1024)S(1)} %multiply_reduce_fusion.1, bf16[2048,2024]{1,0:T(8,128)(2,1)} %all-gather.2.cloned.1.call-done), kind=kOutput, calls=%fused_computation.13 | convolution fusion | flops 17003708416 | bytes 20692992 | tf_op jit(solution)/shard_map/dot_general | solution.py:39
  173.8 2.0 %reduce-precision_convert_fusion = (bf16[1024,1000]{0,1:T(8,128)(2,1)S(1)}, bf16[1024,1000]{0,1:T(8,128)(2,1)S(1)}) fusion(f32[1024,128]{1,0:T(8,128)S(1)} %bitcast.50, f32[128,1000]{1,0:T(8,128)S(1)} %bitcast.48), kind=kOutput, calls=%fused_computation.23 | convolution fusion | flops 790528000 | bytes 5132288 | tf_op jit(solution)/shard_map/dot_general | solution.py:59
  175.8 13.3 %fusion.15 = f32[2048,1000]{0,1:T(8,128)} fusion(f32[2048,1000]{0,1:T(8,128)} %fusion.8, pred[2048,1024]{1,0:T(32,128)(4,1)S(1)} %iota_compare_fusion, bf16[1024,1000]{0,1:T(8,128)(2,1)S(1)} %get-tuple-element.6, bf16[1024,1000]{0,1:T(8,128)(2,1)S(1)} %get-tuple-element.5), kind=kOutput, calls=%fused_computation.26 | convolution fusion | flops 8403042304 | bytes 22577152 | tf_op jit(solution)/shard_map/dot_general | solution.py:64
  (17 shorter events, 0.3 us)
Async XLA Ops:
  6.5 76.6 %all-gather.2.cloned.1.call-start = ((), (), s32[]{:S(2)}) async-start(), calls=%async_computation.7 | async-start | bytes 8912896 | tf_op jit(solution)/shard_map/all_gather | solution.py:31
  30.4 9.8 %all-to-all-start.1 = ((s32[8,128,1]{1,2,0:T(1,128)}), s32[8,128,1]{1,2,0:T(1,128)S(1)}, u32[]{:S(2)}, u32[]{:S(2)}) async-start(s32[8,128,1]{1,2,0:T(1,128)} %bitcast.6), calls=%async_computation.1 | async-start | bytes 8192 | tf_op jit(solution)/shard_map/all_to_all | solution.py:50
  40.3 20.8 %all-to-all-start.2 = ((f32[8,128,128]{2,1,0:T(8,128)}), f32[8,128,128]{2,1,0:T(8,128)S(1)}, u32[]{:S(2)}, u32[]{:S(2)}) async-start(f32[8,128,128]{2,1,0:T(8,128)} %bitcast.8), calls=%async_computation.2 | async-start | bytes 1048576 | tf_op jit(solution)/shard_map/all_to_all | solution.py:51
  101.0 37.2 %copy-start = (f32[128]{0:T(128)S(1)}, f32[128]{0:T(128)}, u32[]{:S(2)}) copy-start(f32[128]{0:T(128)} %param.10) | copy-start | bytes 1540
  121.9 11.9 %all-to-all-start.4 = ((f32[16,1,1000]{2,1,0:T(1,128)}), f32[16,1,1000]{2,1,0:T(1,128)S(1)}, u32[]{:S(2)}, u32[]{:S(2)}) async-start(f32[16,1,1000]{2,1,0:T(1,128)} %all_to_all.51), calls=%async_computation.4 | async-start | bytes 131072 | tf_op jit(solution)/shard_map/all_to_all | solution.py:12
  134.5 9.6 %all-to-all-start.5 = ((f32[16,1,1000]{2,1,0:T(1,128)}), f32[16,1,1000]{2,1,0:T(1,128)S(1)}, u32[]{:S(2)}, u32[]{:S(2)}) async-start(f32[16,1,1000]{2,1,0:T(1,128)} %tile.9), calls=%async_computation.5 | async-start | bytes 131072 | tf_op jit(solution)/shard_map/all_to_all | solution.py:18
  145.0 28.8 %all-to-all-start.6 = ((f32[8,16,1000]{2,1,0:T(8,128)}), f32[8,16,1000]{2,1,0:T(8,128)S(1)}, u32[]{:S(2)}, u32[]{:S(2)}) async-start(f32[8,16,1000]{2,1,0:T(8,128)} %tile.11), calls=%async_computation.6 | async-start | bytes 1048576 | tf_op jit(solution)/shard_map/all_to_all | solution.py:18
Sparse Core Ops, SparseCore 0:
  25.3 57.7 all-gather.1
